TPU v7x, 32 devices: a whole 2x2x4 slice. The times are simulated.
32 devices in a mesh: groups: 2 (over y), replica: 4 (over z), tensor: 4 (over x, core).
Axes of the slice: x: 2, y: 2, z: 4, core: 2. Of those that a mesh axis runs over, the one named last changes fastest.
Arguments:
- queries: bfloat16 [8, 128, 8192], P(('groups', 'replica'), None, 'tensor'), parts along dimension 0, may hold values from -12 to 12
- suffix_kv: bfloat16 [8, 2, 128, 1024], P(('groups', 'replica'), None, None, 'tensor'), parts along dimension 0, may hold values from -12 to 12
- page_pool: bfloat16 [96, 2, 128, 1024], P(('groups', 'replica'), None, 'tensor'), parts along dimension 0, may hold values from -6 to 6
- offsets: int32 [8, 8], P('groups'), parts along dimension 0, may hold values from 1 to 3, as said below
- slots: int32 [8, 8], P('groups'), parts along dimension 0, may hold values from 0 to 11, as said below
- prefix_len: int32 [8], P('groups'), parts along dimension 0, may hold values from 1 to 1024, 2048 in all
Outputs:
- attended: bfloat16 [8, 128, 8192], P(('groups', 'replica'), None, 'tensor'), parts along dimension 0
There are 2 independent parts, one for each index of `groups`. A program takes and returns all parts, laid end to end along the dimension named above; each array names one. Nothing has to cross between parts.
Inputs may be any that keep to these rules, and one draw needn't show every extreme that they name: Page p of request r is held by replica (r - offsets[r, p]) mod 4; one request takes at most 4 pages from one holder, and exactly 4 from some holder. `slots`: the prefix pages of one request are distinct pool entries. `prefix_len`: the longest prefix fills all 8 pages.
All inputs are finite; a program needn't handle non-finite values.
Results may differ from a plain program's by a relative error of at most 0.0034.
Values may be sent and summed in bfloat16 or wider, within the bound.
No kernel may reach another device: no remote copies, remote signals or barrier semaphores. Data moves between devices by JAX's collectives and lax.ppermute only.
A program may use at most 64 MiB of HBM per device.

v0:
```python
import math
import jax
import jax.numpy as jnp
from jax import lax
from jax.sharding import PartitionSpec as P

HEADS = 64
KV_HEADS = 8
HEAD_DIM = 128
NEG_FILL = -1e30


def passed_along(value, axis, steps):
    count = lax.axis_size(axis)
    pairs = [(source, (source + steps) % count) for source in range(count)]
    return lax.ppermute(value, axis, pairs)


def absorb(state_now, scores, visible, values):
    run_max, run_sum, run_acc = state_now
    masked = jnp.where(visible, scores, NEG_FILL)
    new_max = jnp.maximum(run_max, jnp.max(masked, axis=-1))
    weights = jnp.where(visible, jnp.exp(masked - new_max[..., None]), 0.0)
    rescale = jnp.exp(run_max - new_max)
    run_sum = run_sum * rescale + jnp.sum(weights, axis=-1)
    update = jnp.einsum(
        "kgqc,ckd->kgqd", weights.astype(jnp.bfloat16), values, preferred_element_type=jnp.float32
    )
    run_acc = run_acc * rescale[..., None] + update
    return (new_max, run_sum, run_acc)


def pack_pages(pool_part, offsets, slots, holder, replicas, span_count, slot_cap):
    distances = jnp.arange(1, span_count + 1, dtype=jnp.int32)
    readers = (holder + distances) % replicas
    off_rows = jnp.take(offsets, readers, axis=0)
    slot_rows = jnp.take(slots, readers, axis=0)
    matched = (off_rows == distances[:, None]).astype(jnp.int32)
    ranking = jnp.cumsum(matched, axis=1) - 1
    places = jnp.arange(slot_cap, dtype=jnp.int32)
    picked = matched[:, None, :] * (ranking[:, None, :] == places[None, :, None]).astype(jnp.int32)
    chosen = jnp.sum(picked * slot_rows[:, None, :], axis=2)
    gathered = jnp.take(pool_part, chosen.reshape(-1), axis=0)
    return gathered.reshape((span_count, slot_cap) + pool_part.shape[1:])


def page_index(own_offsets, slot_cap):
    page_count = own_offsets.shape[0]
    same_holder = own_offsets[:, None] == own_offsets[None, :]
    counter = jnp.arange(page_count, dtype=jnp.int32)
    earlier = counter[None, :] < counter[:, None]
    ranking = jnp.sum((same_holder & earlier).astype(jnp.int32), axis=1)
    return (own_offsets - 1) * slot_cap + ranking


def on_device(queries, suffix_kv, page_pool, offsets, slots, prefix_len):
    replicas = lax.axis_size("replica")
    reader = lax.axis_index("replica")
    span_count = min(8, replicas - 1)
    page_count = offsets.shape[1]
    slot_cap = (page_count + span_count - 1) // span_count + 1
    own_offsets = lax.dynamic_index_in_dim(offsets, reader, 0, keepdims=False)
    own_length = lax.dynamic_index_in_dim(prefix_len, reader, 0, keepdims=False)
    source = lax.all_to_all(page_pool, "tensor", split_axis=3, concat_axis=2, tiled=True)
    payload = pack_pages(source, offsets, slots, reader, replicas, span_count, slot_cap)
    arrivals = []
    for distance in range(1, span_count + 1):
        arrivals.append(passed_along(payload[distance - 1], "replica", distance))
    arrived = jnp.stack(arrivals)
    flattened = arrived.reshape((span_count * slot_cap,) + arrived.shape[2:])
    fetched = jnp.take(flattened, page_index(own_offsets, slot_cap), axis=0)
    width = fetched.shape[3]
    kv_local = width // HEAD_DIM
    group = HEADS // KV_HEADS
    suffix_rows = queries.shape[1]
    prefix_rows = page_count * fetched.shape[2]
    scale = HEAD_DIM ** (-0.5)
    query_heads = queries[0].reshape(suffix_rows, kv_local, group, HEAD_DIM)
    suffix_keys = suffix_kv[0, 0].reshape(suffix_rows, kv_local, HEAD_DIM)
    suffix_vals = suffix_kv[0, 1].reshape(suffix_rows, kv_local, HEAD_DIM)
    initial = (
        jnp.full((kv_local, group, suffix_rows), NEG_FILL, jnp.float32),
        jnp.zeros((kv_local, group, suffix_rows), jnp.float32),
        jnp.zeros((kv_local, group, suffix_rows, HEAD_DIM), jnp.float32),
    )
    suffix_scores = (
        jnp.einsum("qkgd,ckd->kgqc", query_heads, suffix_keys, preferred_element_type=jnp.float32)
        * scale
    )
    query_pos = jnp.arange(suffix_rows, dtype=jnp.int32)
    causal = query_pos[:, None] >= query_pos[None, :]
    state_now = absorb(initial, suffix_scores, causal, suffix_vals)
    block_rows = math.gcd(prefix_rows, 512)
    block_count = prefix_rows // block_rows
    prefix_keys = fetched[:, 0].reshape(block_count, block_rows, kv_local, HEAD_DIM)
    prefix_vals = fetched[:, 1].reshape(block_count, block_rows, kv_local, HEAD_DIM)
    block_pos = jnp.arange(block_rows, dtype=jnp.int32)

    def visit(state_in, pieces):
        keys_block, vals_block, first_row = pieces
        block_scores = (
            jnp.einsum(
                "qkgd,ckd->kgqc", query_heads, keys_block, preferred_element_type=jnp.float32
            )
            * scale
        )
        visible = first_row + block_pos < own_length
        return (absorb(state_in, block_scores, visible, vals_block), None)

    starts = jnp.arange(block_count, dtype=jnp.int32) * block_rows
    state_now, unused = lax.scan(visit, state_now, (prefix_keys, prefix_vals, starts))
    run_max, run_sum, run_acc = state_now
    result = run_acc / run_sum[..., None]
    result = result.transpose(2, 0, 1, 3).reshape(1, suffix_rows, kv_local * group * HEAD_DIM)
    return result.astype(jnp.bfloat16)


def solution(mesh):
    in_specs = (
        P(("groups", "replica"), None, "tensor"),
        P(("groups", "replica"), None, None, "tensor"),
        P(("groups", "replica"), None, "tensor", None),
        P("groups", None),
        P("groups", None),
        P("groups"),
    )
    out_specs = P(("groups", "replica"), None, "tensor")
    return jax.shard_map(
        on_device, mesh=mesh, in_specs=in_specs, out_specs=out_specs, check_vma=False
    )
```

profile of v0, /device:TPU:9, one launch (start us, length us, event | category | flops | bytes accessed | tf_op | source)
XLA Modules:
  0.0 132.8 jit_solution(631455684307266697)
XLA Ops:
  0.0 0.0 copy-start
  0.0 12.7 %copy.73 = bf16[12,2,32,1024]{2,0,1,3:T(8,128)(2,1)} copy(bf16[12,2,32,1024]{3,2,1,0:T(8,128)(2,1)} %param.12) | data formatting | bytes 3145728 | tf_op args[2]
  12.7 8.9 %reshape.178 = bf16[4,2,98304]{2,1,0:T(2,128)(2,1)} reshape(bf16[1024,2,12,32]{3,2,1,0:T(8,128)(2,1)} %bitcast.95) | data formatting | bytes 3145728
  21.6 4.3 %all-to-all-start = ((bf16[4,2,98304]{2,1,0:T(2,128)(2,1)}), bf16[4,2,98304]{2,1,0:T(2,128)(2,1)S(1)}, u32[]{:S(2)}, u32[]{:S(2)}) async-start(bf16[4,2,98304]{2,1,0:T(2,128)(2,1)} %reshape.178), calls=%async_computation | async-start | bytes 3145728 | tf_op jit(solution)/shard_map/all_to_all | solution.py:64
  25.9 0.0 copy-done.4
  26.0 0.6 gather_fusion.2
  26.5 0.0 copy-done
  26.5 0.6 gather_fusion.3
  27.1 0.1 fusion.28
  27.2 0.2 reduce_window_sum.11
  27.3 0.1 broadcast_select_fusion.2
  27.4 0.1 multiply_reduce_fusion
  27.6 0.1 reshape.134
  27.6 0.1 reshape.133
  27.8 0.2 convert_reduce_fusion
  28.0 0.0 copy-done.2
  28.0 0.3 copy.67
  28.3 0.0 copy-done.5
  28.3 0.1 copy.94
  28.4 0.4 fusion.38
  28.8 0.2 fusion.21
  29.1 16.0 %all-to-all-done = bf16[4,2,98304]{2,1,0:T(2,128)(2,1)S(1)} async-done(((bf16[4,2,98304]{2,1,0:T(2,128)(2,1)}), bf16[4,2,98304]{2,1,0:T(2,128)(2,1)S(1)}, u32[]{:S(2)}, u32[]{:S(2)}) %all-to-all-start) | async-done | bytes 1572896 | tf_op jit(solution)/shard_map/all_to_all | solution.py:64
  45.1 7.1 %reshape.179 = bf16[1024,2,12,32]{3,2,1,0:T(8,128)(2,1)} reshape(bf16[4,2,98304]{2,1,0:T(2,128)(2,1)S(1)} %all-to-all-done) | data formatting | bytes 3145728
  52.2 9.6 %copy.91 = bf16[12,2,32,4,256]{4,3,2,1,0:T(4,128)(2,1)S(1)} copy(bf16[12,2,32,4,256]{2,0,1,4,3:T(8,128)(2,1)} %bitcast.94) | data formatting | bytes 3145728 | tf_op jit(solution)/shard_map/all_to_all | solution.py:64
  61.7 1.5 %copy.75 = bf16[12,2,4,32,256]{4,3,2,1,0:T(8,128)(2,1)} copy(bf16[12,2,4,32,256]{4,2,3,1,0:T(4,128)(2,1)S(1)} %bitcast.96) | data formatting | bytes 3145728 | tf_op jit(solution)/shard_map/all_to_all | solution.py:64
  63.2 2.1 %gather_fusion = bf16[12,2,128,256]{3,2,1,0:T(8,128)(2,1)S(1)} fusion(bf16[12,2,128,256]{3,2,1,0:T(8,128)(2,1)} %bitcast.97, s32[1024]{0:T(1024)S(1)} %pad_clamp_fusion.1), kind=kCustom, calls=%fused_computation.2 | custom fusion | bytes 3145776 | tf_op jit(solution)/shard_map/jit(_take)/gather | solution.py:43
  65.3 0.0 copy-start.6
  65.3 0.2 broadcast_select_fusion
  65.5 1.1 fusion.35
  66.6 1.3 collective-permute-start
  67.9 1.0 collective-permute-start.1
  68.9 1.5 %collective-permute-start.2 = (bf16[4,2,128,256]{3,2,1,0:T(8,128)(2,1)S(1)}, bf16[4,2,128,256]{3,2,1,0:T(8,128)(2,1)}, u32[]{:S(2)}, u32[]{:S(2)}) collective-permute-start(bf16[4,2,128,256]{3,2,1,0:T(8,128)(2,1)S(1)} %get-tuple-element.151), channel_id=1, source_target_pairs={{0,12},{4,0},{8,4},{12,8},{1,13},{5,1},{9,5},{13,9},{2,14},{6,2},{... | collective-permute-start | bytes 1572872 | tf_op jit(solution)/shard_map/ppermute | solution.py:16
  70.4 0.3 copy.77
  70.7 0.1 copy.95
  70.8 0.0 copy-done.6
  70.8 0.6 dynamic_slice.19
  71.4 1.5 %convolution_add_fusion = f32[2,8,128,128]{3,2,1,0:T(8,128)} fusion(bf16[128,2,128,1]{0,2,3,1:T(8,128)(2,1)S(1)} %bitcast.102, f32[2,8,128,128]{2,3,1,0:T(8,128)S(1)} %get-tuple-element.160, f32[2,8,128]{2,1,0:T(8,128)S(1)} %get-tuple-element.157, f32[2,8,128]{2,1,0:T(8,128)S(1)} %broadcast_maximum_fusion, pred[128,128]{0,1:T(8,128)(4,1)S(1)} %iota_compare_fusion), kind=kOutput, calls=%fused_computation.30 | convolution fusion | flops 68157440 | bytes 2195456 | tf_op jit(solution)/shard_map/kgqc,ckd->kgqd/dot_general | solution.py:26
  72.9 6.5 %collective-permute-done = bf16[4,2,128,256]{3,2,1,0:T(8,128)(2,1)S(1)} collective-permute-done((bf16[4,2,128,256]{3,2,1,0:T(8,128)(2,1)}, bf16[4,2,128,256]{3,2,1,0:T(8,128)(2,1)S(1)}, u32[]{:S(2)}, u32[]{:S(2)}) %collective-permute-start) | collective-permute-done | bytes 524320 | tf_op jit(solution)/shard_map/ppermute | solution.py:16
  79.4 32.9 %collective-permute-done.1 = bf16[4,2,128,256]{3,2,1,0:T(8,128)(2,1)} collective-permute-done((bf16[4,2,128,256]{3,2,1,0:T(8,128)(2,1)}, bf16[4,2,128,256]{3,2,1,0:T(8,128)(2,1)}, u32[]{:S(2)}, u32[]{:S(2)}) %collective-permute-start.1) | collective-permute-done | bytes 524320 | tf_op jit(solution)/shard_map/ppermute | solution.py:16
  112.3 3.1 %collective-permute-done.2 = bf16[4,2,128,256]{3,2,1,0:T(8,128)(2,1)} collective-permute-done((bf16[4,2,128,256]{3,2,1,0:T(8,128)(2,1)S(1)}, bf16[4,2,128,256]{3,2,1,0:T(8,128)(2,1)}, u32[]{:S(2)}, u32[]{:S(2)}) %collective-permute-start.2) | collective-permute-done | bytes 524320 | tf_op jit(solution)/shard_map/ppermute | solution.py:16
  115.4 0.0 copy-done.3
  115.4 1.5 %pad_maximum_fusion = bf16[3,4,2,128,256]{4,3,2,1,0:T(8,128)(2,1)S(1)} fusion(bf16[1,4,2,128,256]{4,3,2,1,0:T(8,128)(2,1)} %bitcast.14, bf16[1,4,2,128,256]{4,3,2,1,0:T(8,128)(2,1)} %bitcast.13, bf16[1,4,2,128,256]{4,3,2,1,0:T(8,128)(2,1)} %bitcast.101), kind=kLoop, calls=%fused_computation.28 | loop fusion | flops 1572864 | bytes 3145728 | tf_op jit(solution)/shard_map/stack | solution.py:69
  116.9 0.6 gather_fusion.1
  117.5 0.2 broadcast_select_fusion.1
  117.7 0.1 fusion.36
  117.8 0.1 reshape_squeeze.18
  117.9 0.1 reshape_squeeze.19
  118.1 0.8 copy-done.1
  118.9 12.1 %while.15 = (s32[]{:T(128)}, f32[2,8,128]{2,1,0:T(8,128)S(1)}, f32[2,8,128]{2,1,0:T(8,128)S(1)}, f32[2,8,128,128]{3,2,1,0:T(8,128)S(1)}, s32[2]{0:T(128)S(1)}, /...) while((s32[]{:T(128)}, f32[2,8,128]{2,1,0:T(8,128)S(1)}, ...), condition=%wide.region_8.10_spmd.clone, body=%wide.region_5.9_spmd.clone.sunk | while | flops 551031808 | bytes 16910460 | solution.py:111
  118.9 0.6 dynamic_slice.36
  119.5 1.2 fusion.50
  120.7 0.4 constant_dynamic-slice_fusion.4
  121.1 0.8 bitcast_reduce_fusion.2
  121.9 1.1 fusion.51
  123.1 1.9 %fusion.52 = f32[2,8,128,128]{3,2,1,0:T(8,128)S(1)} fusion(f32[2,512,128,8]{2,1,3,0:T(8,128)S(1)} %get-tuple-element.226, f32[2,8,128]{2,1,0:T(8,128)S(1)} %max.5, pred[512]{0:T(512)(128)(4,1)S(1)} %fusion.50, f32[2,8,128,128]{3,2,1,0:T(8,128)S(1)} %get-tuple-element.243, f32[2,8,128]{2,1,0:T(8,128)S(1)} %get-tuple-element.228, ...), kind=kOutput, calls=%fused_computation.15.clone.1 | convolution fusion | flops 274202624 | bytes 6570496 | tf_op jit(solution)/shard_map/while/body/eval_jaxpr/kgqc,ckd->kgqd/dot_general | solution.py:26
  125.0 0.6 dynamic_slice.36
  125.6 1.2 fusion.50
  126.8 0.4 constant_dynamic-slice_fusion.4
  127.2 0.8 bitcast_reduce_fusion.2
  127.9 1.1 fusion.51
  129.1 1.9 %fusion.52 = f32[2,8,128,128]{3,2,1,0:T(8,128)S(1)} fusion(f32[2,512,128,8]{2,1,3,0:T(8,128)S(1)} %get-tuple-element.226, f32[2,8,128]{2,1,0:T(8,128)S(1)} %max.5, pred[512]{0:T(512)(128)(4,1)S(1)} %fusion.50, f32[2,8,128,128]{3,2,1,0:T(8,128)S(1)} %get-tuple-element.243, f32[2,8,128]{2,1,0:T(8,128)S(1)} %get-tuple-element.228, ...), kind=kOutput, calls=%fused_computation.15.clone.1 | convolution fusion | flops 274202624 | bytes 6570496 | tf_op jit(solution)/shard_map/while/body/eval_jaxpr/kgqc,ckd->kgqd/dot_general | solution.py:26
  131.0 0.3 fusion.25
  131.4 0.3 copy.79
  131.7 1.0 convert_element_type.35
  (27 shorter events, 0.2 us)
Async XLA Ops:
  0.0 26.5 %copy-start = (s32[4,8]{1,0:T(4,128)S(1)}, s32[4,8]{1,0:T(4,128)}, u32[]{:S(2)}) copy-start(s32[4,8]{1,0:T(4,128)} %param.14) | copy-start | bytes 388
  12.7 13.3 %copy-start.4 = (s32[4,8]{1,0:T(4,128)S(1)}, s32[4,8]{1,0:T(4,128)}, u32[]{:S(2)}) copy-start(s32[4,8]{1,0:T(4,128)} %param.13) | copy-start | bytes 388
  12.7 15.3 %copy-start.2 = (bf16[1,128,2048]{2,1,0:T(8,128)(2,1)S(1)}, bf16[1,128,2048]{2,1,0:T(8,128)(2,1)}, u32[]{:S(2)}) copy-start(bf16[1,128,2048]{2,1,0:T(8,128)(2,1)} %param.10) | copy-start | bytes 1572868
  21.6 6.7 %copy-start.5 = (bf16[1,2,128,256]{3,2,1,0:T(8,128)(2,1)S(1)}, bf16[1,2,128,256]{3,2,1,0:T(8,128)(2,1)}, u32[]{:S(2)}) copy-start(bf16[1,2,128,256]{3,2,1,0:T(8,128)(2,1)} %param.11) | copy-start | bytes 393220
  21.6 23.6 %all-to-all-start = ((bf16[4,2,98304]{2,1,0:T(2,128)(2,1)}), bf16[4,2,98304]{2,1,0:T(2,128)(2,1)S(1)}, u32[]{:S(2)}, u32[]{:S(2)}) async-start(bf16[4,2,98304]{2,1,0:T(2,128)(2,1)} %reshape.178), calls=%async_computation | async-start | bytes 3145728 | tf_op jit(solution)/shard_map/all_to_all | solution.py:64
  65.3 5.5 %copy-start.6 = (s32[4]{0:T(128)S(1)}, s32[4]{0:T(128)}, u32[]{:S(2)}) copy-start(s32[4]{0:T(128)} %param.15) | copy-start | bytes 52
  66.6 12.8 %collective-permute-start = (bf16[4,2,128,256]{3,2,1,0:T(8,128)(2,1)}, bf16[4,2,128,256]{3,2,1,0:T(8,128)(2,1)S(1)}, u32[]{:S(2)}, u32[]{:S(2)}) collective-permute-start(bf16[4,2,128,256]{3,2,1,0:T(8,128)(2,1)} %get-tuple-element.150), channel_id=1, source_target_pairs={{0,4},{4,8},{8,12},{12,0},{1,5},{5,9},{9,13},{13,1},{2,6},{6,10},{... | collective-permute-start | bytes 1572872 | tf_op jit(solution)/shard_map/ppermute | solution.py:16
  67.9 44.4 %collective-permute-start.1 = (bf16[4,2,128,256]{3,2,1,0:T(8,128)(2,1)}, bf16[4,2,128,256]{3,2,1,0:T(8,128)(2,1)}, u32[]{:S(2)}, u32[]{:S(2)}) collective-permute-start(bf16[4,2,128,256]{3,2,1,0:T(8,128)(2,1)} %get-tuple-element.152), channel_id=1, source_target_pairs={{0,8},{4,12},{8,0},{12,4},{1,9},{5,13},{9,1},{13,5},{2,10},{6,14},... | collective-permute-start | bytes 1572872 | tf_op jit(solution)/shard_map/ppermute | solution.py:16
  68.9 46.4 %collective-permute-start.2 = (bf16[4,2,128,256]{3,2,1,0:T(8,128)(2,1)S(1)}, bf16[4,2,128,256]{3,2,1,0:T(8,128)(2,1)}, u32[]{:S(2)}, u32[]{:S(2)}) collective-permute-start(bf16[4,2,128,256]{3,2,1,0:T(8,128)(2,1)S(1)} %get-tuple-element.151), channel_id=1, source_target_pairs={{0,12},{4,0},{8,4},{12,8},{1,13},{5,1},{9,5},{13,9},{2,14},{6,2},{... | collective-permute-start | bytes 1572872 | tf_op jit(solution)/shard_map/ppermute | solution.py:16
  79.4 36.0 %copy-start.3 = (bf16[4,2,128,256]{3,2,1,0:T(8,128)(2,1)}, bf16[4,2,128,256]{3,2,1,0:T(8,128)(2,1)S(1)}, u32[]{:S(2)}) copy-start(bf16[4,2,128,256]{3,2,1,0:T(8,128)(2,1)S(1)} %collective-permute-done) | copy-start | bytes 1572868
  117.7 1.2 copy-start.1
where the time goes:
time: 133 us
  waiting for transfers between devices  58.5 us (44%)
  local copies, waits for them, and re-layouts  50.6 us (38%)
  starting transfers between devices  8.11 us (6%)
  other arithmetic  7.99 us (6%)
  matrix products  7.18 us (5%)
    ppermute x3, waiting for transfers between devices, passed_along(): return lax.ppermute(value, axis, pairs)  42.4 us
    unnamed x21, local copies, waits for them, and re-layouts  30.3 us
    all_to_all x1, waiting for transfers between devices, on_device(): lax.all_to_all(page_pool, 'tensor', split_axis=3, concat_axis=2, tiled=True)  16 us
    all_to_all x2, local copies, waits for them, and re-layouts, on_device(): lax.all_to_all(page_pool, 'tensor', split_axis=3, concat_axis=2, tiled=True)  11 us
    dot_general x3, matrix products, absorb(): jnp.einsum('kgqc,ckd->kgqd', weights.astype(jnp.bfloat16), values, prefer...  5.31 us
    all_to_all x1, starting transfers between devices, on_device(): lax.all_to_all(page_pool, 'tensor', split_axis=3, concat_axis=2, tiled=True)  4.34 us
    ppermute x3, starting transfers between devices, passed_along(): return lax.ppermute(value, axis, pairs)  3.78 us
  transfers between devices with their start and end apart: 4, of which 4 were waited for; matrix products, arithmetic and copies ran while one was open for 4% of the time, Pallas kernels for 0%

commit v1 on v0

--- a/solution.py
+++ b/solution.py
@@ -61,7 +61,12 @@
     slot_cap = (page_count + span_count - 1) // span_count + 1
     own_offsets = lax.dynamic_index_in_dim(offsets, reader, 0, keepdims=False)
     own_length = lax.dynamic_index_in_dim(prefix_len, reader, 0, keepdims=False)
-    source = lax.all_to_all(page_pool, "tensor", split_axis=3, concat_axis=2, tiled=True)
+    source = jnp.concatenate(
+        lax.all_to_all(
+            jnp.stack(jnp.split(page_pool, lax.axis_size("tensor"), axis=3)), "tensor", 0, 0
+        ),
+        axis=2,
+    )
     payload = pack_pages(source, offsets, slots, reader, replicas, span_count, slot_cap)
     arrivals = []
     for distance in range(1, span_count + 1):

time: 133 us -> 100 us (0.75)
  the two profiles are of different devices: /device:TPU:9 before, /device:TPU:0 now
where the time goes in v1:
time: 100 us; the launch traced here: 99.9 us
  waiting for transfers between devices  59 us (59%)
  local copies, waits for them, and re-layouts  13.9 us (14%)
  starting transfers between devices  9.73 us (10%)
  other arithmetic  9.64 us (10%)
  matrix products  7.19 us (7%)
    ppermute x3, waiting for transfers between devices, passed_along(): return lax.ppermute(value, axis, pairs)  42.1 us
    all_to_all x1, waiting for transfers between devices, on_device(): lax.all_to_all(jnp.stack(jnp.split(page_pool, lax.axis_size('tensor'), ax...  16.9 us
    ppermute x3, starting transfers between devices, passed_along(): return lax.ppermute(value, axis, pairs)  5.39 us
    dot_general x3, matrix products, absorb(): jnp.einsum('kgqc,ckd->kgqd', weights.astype(jnp.bfloat16), values, prefer...  5.32 us
    all_to_all x1, starting transfers between devices, on_device(): lax.all_to_all(jnp.stack(jnp.split(page_pool, lax.axis_size('tensor'), ax...  4.34 us
    lt x2, other arithmetic, visit(): visible = first_row + block_pos < own_length  2.68 us
    reduce_sum x3, other arithmetic, absorb(): run_sum = run_sum * rescale + jnp.sum(weights, axis=-1)  2.51 us
    gather x1, local copies, waits for them, and re-layouts, pack_pages(): gathered = jnp.take(pool_part, chosen.reshape(-1), axis=0)  2.05 us
  transfers between devices with their start and end apart: 4, of which 4 were waited for; matrix products, arithmetic and copies ran while one was open for 6% of the time, Pallas kernels for 0%

profile of v1, /device:TPU:0, one launch (start us, length us, event | category | flops | bytes accessed | tf_op | source)
XLA Modules:
  0.0 99.9 jit_solution(11257995626010672255)
XLA Ops:
  0.0 0.0 copy-start
  0.0 1.6 %slice_bitcast_fusion.3 = (bf16[1,12,2,32,256]{4,3,2,1,0:T(8,128)(2,1)S(1)}, bf16[1,12,2,32,256]{4,3,2,1,0:T(8,128)(2,1)S(1)}, bf16[1,12,2,32,256]{4,3,2,1,0:T(8,128)(2,1)S(1)}, bf16[1,12,2,32,256]{4,3,2,1,0:T(8,128)(2,1)S(1)}) fusion(bf16[12,2,32,1024]{3,2,1,0:T(8,128)(2,1)} %param.12), kind=kLoop, calls=%fused_computation.47 | loop fusion | bytes 3145728 | tf_op jit(solution)/shard_map/stack | solution.py:66
  1.6 1.4 %pad_maximum_fusion = bf16[4,12,2,32,256]{4,3,2,1,0:T(8,128)(2,1)} fusion(bf16[1,12,2,32,256]{4,3,2,1,0:T(8,128)(2,1)S(1)} %get-tuple-element.146, bf16[1,12,2,32,256]{4,3,2,1,0:T(8,128)(2,1)S(1)} %get-tuple-element.147, bf16[1,12,2,32,256]{4,3,2,1,0:T(8,128)(2,1)S(1)} %get-tuple-element.145, bf16[1,12,2,32,256]{4,3,2,1,0:T(8,128)(2,1)S(1)} %get-tuple-element.144), kind=kLoop, calls=%fused_computation.28 | loop fusion | flops 2359296 | bytes 3145728 | tf_op jit(solution)/shard_map/stack | solution.py:66
  2.9 0.0 copy-start.4
  2.9 4.3 %all-to-all-start = ((bf16[4,12,2,32,256]{4,3,2,1,0:T(8,128)(2,1)}), bf16[4,12,2,32,256]{4,3,2,1,0:T(8,128)(2,1)S(1)}, u32[]{:S(2)}, u32[]{:S(2)}) async-start(bf16[4,12,2,32,256]{4,3,2,1,0:T(8,128)(2,1)} %pad_maximum_fusion), calls=%async_computation | async-start | bytes 3145728 | tf_op jit(solution)/shard_map/all_to_all | solution.py:65
  7.3 0.0 copy-done
  7.3 0.6 gather_fusion.3
  7.9 0.0 copy-done.4
  7.9 0.6 gather_fusion.2
  8.5 0.1 fusion.28
  8.5 0.2 reduce_window_sum.11
  8.7 0.1 broadcast_select_fusion.2
  8.8 0.1 multiply_reduce_fusion
  9.0 0.1 reshape.142
  9.0 0.1 reshape.139
  9.2 0.2 convert_reduce_fusion
  9.4 0.0 copy-done.5
  9.4 0.1 copy.73
  9.5 0.0 copy-done.2
  9.5 0.3 copy.49
  9.8 0.4 fusion.38
  10.2 0.2 fusion.21
  10.5 16.9 %all-to-all-done = bf16[4,12,2,32,256]{4,3,2,1,0:T(8,128)(2,1)S(1)} async-done(((bf16[4,12,2,32,256]{4,3,2,1,0:T(8,128)(2,1)}), bf16[4,12,2,32,256]{4,3,2,1,0:T(8,128)(2,1)S(1)}, u32[]{:S(2)}, u32[]{:S(2)}) %all-to-all-start) | async-done | bytes 1572896 | tf_op jit(solution)/shard_map/all_to_all | solution.py:65
  27.4 1.3 %copy.55 = bf16[4,12,2,32,256]{4,3,0,2,1:T(8,128)(2,1)} copy(bf16[4,12,2,32,256]{4,3,2,1,0:T(8,128)(2,1)S(1)} %all-to-all-done) | data formatting | bytes 3145728 | tf_op jit(solution)/shard_map/all_to_all | solution.py:65
  28.7 2.1 %gather_fusion = bf16[12,2,128,256]{3,2,1,0:T(8,128)(2,1)S(1)} fusion(bf16[12,2,128,256]{3,2,1,0:T(8,128)(2,1)} %bitcast.100, s32[1024]{0:T(1024)S(1)} %pad_clamp_fusion.1), kind=kCustom, calls=%fused_computation.2 | custom fusion | bytes 3145776 | tf_op jit(solution)/shard_map/jit(_take)/gather | solution.py:43
  30.8 0.2 broadcast_select_fusion
  31.0 0.0 copy-start.6
  31.0 1.1 %fusion.35 = (bf16[4,2,128,256]{3,2,1,0:T(8,128)(2,1)}, bf16[4,2,128,256]{3,2,1,0:T(8,128)(2,1)}, bf16[4,2,128,256]{3,2,1,0:T(8,128)(2,1)S(1)}) fusion(bf16[12,2,128,256]{3,2,1,0:T(8,128)(2,1)S(1)} %broadcast_select_fusion), kind=kLoop, calls=%fused_computation.84 | loop fusion | bytes 3145728 | tf_op jit(solution)/shard_map/slice | solution.py:73
  32.1 2.3 %collective-permute-start = (bf16[4,2,128,256]{3,2,1,0:T(8,128)(2,1)}, bf16[4,2,128,256]{3,2,1,0:T(8,128)(2,1)S(1)}, u32[]{:S(2)}, u32[]{:S(2)}) collective-permute-start(bf16[4,2,128,256]{3,2,1,0:T(8,128)(2,1)} %get-tuple-element.141), channel_id=1, source_target_pairs={{0,4},{4,8},{8,12},{12,0},{1,5},{5,9},{9,13},{13,1},{2,6},{6,10},{... | collective-permute-start | bytes 1572872 | tf_op jit(solution)/shard_map/ppermute | solution.py:16
  34.4 2.0 %collective-permute-start.2 = (bf16[4,2,128,256]{3,2,1,0:T(8,128)(2,1)}, bf16[4,2,128,256]{3,2,1,0:T(8,128)(2,1)}, u32[]{:S(2)}, u32[]{:S(2)}) collective-permute-start(bf16[4,2,128,256]{3,2,1,0:T(8,128)(2,1)} %get-tuple-element.142), channel_id=1, source_target_pairs={{0,12},{4,0},{8,4},{12,8},{1,13},{5,1},{9,5},{13,9},{2,14},{6,2},{... | collective-permute-start | bytes 1572872 | tf_op jit(solution)/shard_map/ppermute | solution.py:16
  36.5 1.0 %collective-permute-start.1 = (bf16[4,2,128,256]{3,2,1,0:T(8,128)(2,1)S(1)}, bf16[4,2,128,256]{3,2,1,0:T(8,128)(2,1)}, u32[]{:S(2)}, u32[]{:S(2)}) collective-permute-start(bf16[4,2,128,256]{3,2,1,0:T(8,128)(2,1)S(1)} %get-tuple-element.143), channel_id=1, source_target_pairs={{0,8},{4,12},{8,0},{12,4},{1,9},{5,13},{9,1},{13,5},{2,10},{6,14},... | collective-permute-start | bytes 1572872 | tf_op jit(solution)/shard_map/ppermute | solution.py:16
  37.5 0.3 copy.57
  37.8 0.0 copy-done.6
  37.8 0.7 dynamic_slice.19
  38.5 0.1 copy.74
  38.6 1.5 %convolution_add_fusion = f32[2,8,128,128]{3,2,1,0:T(8,128)} fusion(bf16[128,2,128,1]{0,2,3,1:T(8,128)(2,1)S(1)} %bitcast.105, f32[2,8,128,128]{2,3,1,0:T(8,128)S(1)} %get-tuple-element.155, f32[2,8,128]{2,1,0:T(8,128)S(1)} %get-tuple-element.152, f32[2,8,128]{2,1,0:T(8,128)S(1)} %broadcast_maximum_fusion, pred[128,128]{0,1:T(8,128)(4,1)S(1)} %iota_compare_fusion), kind=kOutput, calls=%fused_computation.31 | convolution fusion | flops 68157440 | bytes 2195456 | tf_op jit(solution)/shard_map/kgqc,ckd->kgqd/dot_general | solution.py:26
  40.1 9.4 %collective-permute-done = bf16[4,2,128,256]{3,2,1,0:T(8,128)(2,1)S(1)} collective-permute-done((bf16[4,2,128,256]{3,2,1,0:T(8,128)(2,1)}, bf16[4,2,128,256]{3,2,1,0:T(8,128)(2,1)S(1)}, u32[]{:S(2)}, u32[]{:S(2)}) %collective-permute-start) | collective-permute-done | bytes 524320 | tf_op jit(solution)/shard_map/ppermute | solution.py:16
  49.5 9.7 %collective-permute-done.2 = bf16[4,2,128,256]{3,2,1,0:T(8,128)(2,1)} collective-permute-done((bf16[4,2,128,256]{3,2,1,0:T(8,128)(2,1)}, bf16[4,2,128,256]{3,2,1,0:T(8,128)(2,1)}, u32[]{:S(2)}, u32[]{:S(2)}) %collective-permute-start.2) | collective-permute-done | bytes 524320 | tf_op jit(solution)/shard_map/ppermute | solution.py:16
  59.2 23.0 %collective-permute-done.1 = bf16[4,2,128,256]{3,2,1,0:T(8,128)(2,1)} collective-permute-done((bf16[4,2,128,256]{3,2,1,0:T(8,128)(2,1)S(1)}, bf16[4,2,128,256]{3,2,1,0:T(8,128)(2,1)}, u32[]{:S(2)}, u32[]{:S(2)}) %collective-permute-start.1) | collective-permute-done | bytes 524320 | tf_op jit(solution)/shard_map/ppermute | solution.py:16
  82.2 0.0 copy-done.3
  82.2 1.5 %pad_maximum_fusion.1 = bf16[3,4,2,128,256]{4,3,2,1,0:T(8,128)(2,1)S(1)} fusion(bf16[1,4,2,128,256]{4,3,2,1,0:T(8,128)(2,1)} %bitcast.17, bf16[1,4,2,128,256]{4,3,2,1,0:T(8,128)(2,1)} %bitcast.16, bf16[1,4,2,128,256]{4,3,2,1,0:T(8,128)(2,1)} %bitcast.104), kind=kLoop, calls=%fused_computation.29 | loop fusion | flops 1572864 | bytes 3145728 | tf_op jit(solution)/shard_map/stack | solution.py:74
  83.7 0.6 gather_fusion.1
  84.4 0.2 broadcast_select_fusion.1
  84.5 0.0 copy-start.1
  84.5 0.1 fusion.36
  84.6 0.1 reshape_squeeze.19
  84.8 0.1 reshape_squeeze.18
  84.9 0.9 copy-done.1
  85.8 12.4 %while.15 = (s32[]{:T(128)}, f32[2,8,128]{2,1,0:T(8,128)S(1)}, f32[2,8,128]{2,1,0:T(8,128)S(1)}, f32[2,8,128,128]{3,2,1,0:T(8,128)S(1)}, s32[2]{0:T(128)S(1)}, /...) while((s32[]{:T(128)}, f32[2,8,128]{2,1,0:T(8,128)S(1)}, ...), condition=%wide.region_8.10_spmd.clone, body=%wide.region_5.9_spmd.clone.sunk | while | flops 551031808 | bytes 16910468 | solution.py:116
  85.8 0.6 dynamic_slice.36
  86.3 1.3 %fusion.50 = pred[512]{0:T(512)(128)(4,1)S(1)} fusion(s32[]{:T(128)} %get-tuple-element.250, s32[]{:T(128)} %bitcast.99), kind=kLoop, calls=%fused_computation.22.clone.1 | loop fusion | flops 1024 | bytes 520 | tf_op jit(solution)/shard_map/while/body/eval_jaxpr/lt | solution.py:112
  87.7 0.4 constant_dynamic-slice_fusion.4
  88.1 0.8 bitcast_reduce_fusion.2
  88.8 1.2 %fusion.51 = f32[2,8,128]{2,1,0:T(8,128)S(1)} fusion(f32[2,512,128,8]{2,1,3,0:T(8,128)S(1)} %get-tuple-element.221, f32[2,8,128]{2,1,0:T(8,128)S(1)} %max.5, pred[512]{0:T(512)(128)(4,1)S(1)} %fusion.50), kind=kLoop, calls=%fused_computation.11.clone.1 | loop fusion | flops 5240832 | bytes 4211200 | tf_op jit(solution)/shard_map/while/body/eval_jaxpr/reduce_sum | solution.py:25
  90.0 1.9 %fusion.52 = f32[2,8,128,128]{3,2,1,0:T(8,128)S(1)} fusion(f32[2,512,128,8]{2,1,3,0:T(8,128)S(1)} %get-tuple-element.221, f32[2,8,128]{2,1,0:T(8,128)S(1)} %max.5, pred[512]{0:T(512)(128)(4,1)S(1)} %fusion.50, f32[2,8,128,128]{3,2,1,0:T(8,128)S(1)} %get-tuple-element.238, f32[2,8,128]{2,1,0:T(8,128)S(1)} %get-tuple-element.223, ...), kind=kOutput, calls=%fused_computation.15.clone.1 | convolution fusion | flops 274202624 | bytes 6570496 | tf_op jit(solution)/shard_map/while/body/eval_jaxpr/kgqc,ckd->kgqd/dot_general | solution.py:26
  92.0 0.6 dynamic_slice.36
  92.5 1.3 %fusion.50 = pred[512]{0:T(512)(128)(4,1)S(1)} fusion(s32[]{:T(128)} %get-tuple-element.250, s32[]{:T(128)} %bitcast.99), kind=kLoop, calls=%fused_computation.22.clone.1 | loop fusion | flops 1024 | bytes 520 | tf_op jit(solution)/shard_map/while/body/eval_jaxpr/lt | solution.py:112
  93.9 0.4 constant_dynamic-slice_fusion.4
  94.3 0.8 bitcast_reduce_fusion.2
  95.0 1.2 %fusion.51 = f32[2,8,128]{2,1,0:T(8,128)S(1)} fusion(f32[2,512,128,8]{2,1,3,0:T(8,128)S(1)} %get-tuple-element.221, f32[2,8,128]{2,1,0:T(8,128)S(1)} %max.5, pred[512]{0:T(512)(128)(4,1)S(1)} %fusion.50), kind=kLoop, calls=%fused_computation.11.clone.1 | loop fusion | flops 5240832 | bytes 4211200 | tf_op jit(solution)/shard_map/while/body/eval_jaxpr/reduce_sum | solution.py:25
  96.2 1.9 %fusion.52 = f32[2,8,128,128]{3,2,1,0:T(8,128)S(1)} fusion(f32[2,512,128,8]{2,1,3,0:T(8,128)S(1)} %get-tuple-element.221, f32[2,8,128]{2,1,0:T(8,128)S(1)} %max.5, pred[512]{0:T(512)(128)(4,1)S(1)} %fusion.50, f32[2,8,128,128]{3,2,1,0:T(8,128)S(1)} %get-tuple-element.238, f32[2,8,128]{2,1,0:T(8,128)S(1)} %get-tuple-element.223, ...), kind=kOutput, calls=%fused_computation.15.clone.1 | convolution fusion | flops 274202624 | bytes 6570496 | tf_op jit(solution)/shard_map/while/body/eval_jaxpr/kgqc,ckd->kgqd/dot_general | solution.py:26
  98.2 0.3 fusion.25
  98.5 0.3 copy.59
  98.9 1.0 %convert_element_type.35 = bf16[1,128,2048]{2,1,0:T(8,128)(2,1)} reshape(bf16[128,2,8,128]{3,2,1,0:T(8,128)(2,1)S(1)} %copy.59) | data formatting | bytes 1048576 | tf_op jit(solution)/shard_map/convert_element_type | solution.py:120
  (25 shorter events, 0.2 us)
Async XLA Ops:
  0.0 7.3 %copy-start = (s32[4,8]{1,0:T(4,128)S(1)}, s32[4,8]{1,0:T(4,128)}, u32[]{:S(2)}) copy-start(s32[4,8]{1,0:T(4,128)} %param.14) | copy-start | bytes 388
  2.9 5.0 %copy-start.4 = (s32[4,8]{1,0:T(4,128)S(1)}, s32[4,8]{1,0:T(4,128)}, u32[]{:S(2)}) copy-start(s32[4,8]{1,0:T(4,128)} %param.13) | copy-start | bytes 388
  2.9 6.5 %copy-start.5 = (bf16[1,2,128,256]{3,2,1,0:T(8,128)(2,1)S(1)}, bf16[1,2,128,256]{3,2,1,0:T(8,128)(2,1)}, u32[]{:S(2)}) copy-start(bf16[1,2,128,256]{3,2,1,0:T(8,128)(2,1)} %param.11) | copy-start | bytes 393220
  2.9 6.6 %copy-start.2 = (bf16[1,128,2048]{2,1,0:T(8,128)(2,1)S(1)}, bf16[1,128,2048]{2,1,0:T(8,128)(2,1)}, u32[]{:S(2)}) copy-start(bf16[1,128,2048]{2,1,0:T(8,128)(2,1)} %param.10) | copy-start | bytes 1572868
  2.9 24.4 %all-to-all-start = ((bf16[4,12,2,32,256]{4,3,2,1,0:T(8,128)(2,1)}), bf16[4,12,2,32,256]{4,3,2,1,0:T(8,128)(2,1)S(1)}, u32[]{:S(2)}, u32[]{:S(2)}) async-start(bf16[4,12,2,32,256]{4,3,2,1,0:T(8,128)(2,1)} %pad_maximum_fusion), calls=%async_computation | async-start | bytes 3145728 | tf_op jit(solution)/shard_map/all_to_all | solution.py:65
  31.0 6.8 %copy-start.6 = (s32[4]{0:T(128)S(1)}, s32[4]{0:T(128)}, u32[]{:S(2)}) copy-start(s32[4]{0:T(128)} %param.15) | copy-start | bytes 52
  32.1 17.4 %collective-permute-start = (bf16[4,2,128,256]{3,2,1,0:T(8,128)(2,1)}, bf16[4,2,128,256]{3,2,1,0:T(8,128)(2,1)S(1)}, u32[]{:S(2)}, u32[]{:S(2)}) collective-permute-start(bf16[4,2,128,256]{3,2,1,0:T(8,128)(2,1)} %get-tuple-element.141), channel_id=1, source_target_pairs={{0,4},{4,8},{8,12},{12,0},{1,5},{5,9},{9,13},{13,1},{2,6},{6,10},{... | collective-permute-start | bytes 1572872 | tf_op jit(solution)/shard_map/ppermute | solution.py:16
  34.4 24.7 %collective-permute-start.2 = (bf16[4,2,128,256]{3,2,1,0:T(8,128)(2,1)}, bf16[4,2,128,256]{3,2,1,0:T(8,128)(2,1)}, u32[]{:S(2)}, u32[]{:S(2)}) collective-permute-start(bf16[4,2,128,256]{3,2,1,0:T(8,128)(2,1)} %get-tuple-element.142), channel_id=1, source_target_pairs={{0,12},{4,0},{8,4},{12,8},{1,13},{5,1},{9,5},{13,9},{2,14},{6,2},{... | collective-permute-start | bytes 1572872 | tf_op jit(solution)/shard_map/ppermute | solution.py:16
  36.5 45.7 %collective-permute-start.1 = (bf16[4,2,128,256]{3,2,1,0:T(8,128)(2,1)S(1)}, bf16[4,2,128,256]{3,2,1,0:T(8,128)(2,1)}, u32[]{:S(2)}, u32[]{:S(2)}) collective-permute-start(bf16[4,2,128,256]{3,2,1,0:T(8,128)(2,1)S(1)} %get-tuple-element.143), channel_id=1, source_target_pairs={{0,8},{4,12},{8,0},{12,4},{1,9},{5,13},{9,1},{13,5},{2,10},{6,14},... | collective-permute-start | bytes 1572872 | tf_op jit(solution)/shard_map/ppermute | solution.py:16
  49.5 32.7 %copy-start.3 = (bf16[4,2,128,256]{3,2,1,0:T(8,128)(2,1)}, bf16[4,2,128,256]{3,2,1,0:T(8,128)(2,1)S(1)}, u32[]{:S(2)}) copy-start(bf16[4,2,128,256]{3,2,1,0:T(8,128)(2,1)S(1)} %collective-permute-done) | copy-start | bytes 1572868
  84.5 1.2 %copy-start.1 = (f32[2,8,128,128]{3,2,1,0:T(8,128)S(1)}, f32[2,8,128,128]{3,2,1,0:T(8,128)}, u32[]{:S(2)}) copy-start(f32[2,8,128,128]{3,2,1,0:T(8,128)} %convolution_add_fusion) | copy-start | bytes 3145732
